TPU v7x, 256 devices: a whole 4x4x8 slice. The times are simulated.
256 devices in a mesh: rows: 32 (over x, z_lo, y), cols: 8 (over z_hi, core).
Axes of the slice: x: 4, y: 4, z: 8 (z_hi: 4, z_lo: 2; z = z_hi * 2 + z_lo), core: 2. Of those that a mesh axis runs over, the one named last changes fastest.
Arguments:
- state: float32 [9, 1024, 4096], P(None, 'rows', 'cols'), may hold values from -3.5 to 7.2, as said below
- hardness: int32 [1024, 4096], P('rows', 'cols'), may hold values from 0 to 3
- rain_mask: int32 [1024, 4096], P('rows', 'cols'), may hold values from 0 to 1
Outputs:
- final_state: float32 [9, 1024, 4096], P(None, 'rows', 'cols')
Inputs may be any that keep to these rules, and one draw needn't show every extreme that they name: `state`: water depth, sediment and outflows are nonnegative.
All inputs are finite; a program needn't handle non-finite values.
Results may differ from a plain program's by a relative error of at most 0.0003.
Values sent between devices are 32-bit elements; how exact they have to be, the bound alone decides.
No kernel may reach another device: no remote copies, remote signals or barrier semaphores. Data moves between devices by JAX's collectives and lax.ppermute only.
A program may use at most 64 MiB of HBM per device.

v0:
```python
import jax
import jax.numpy as jnp
from jax import lax
from jax.sharding import PartitionSpec as P

STEPS = 8


time_step = 0.25
wet_floor = 0.05
deep_floor = 0.1
carry_coef = 0.4
cap_floor = 0.0025
erode_coef = 0.3
settle_coef = 0.3
slide_coef = 0.1
talus_drop = 0.5
talus_sharp = 4.0
evap_coef = 0.05
rain_depth = 0.1
rock_rates = (1.0, 0.6, 0.3, 0.12)


def with_halo(x, sides, width):
    for axis, dim in sides:
        count, length = (lax.axis_size(axis), x.shape[dim])
        up = [(i, (i + 1) % count) for i in range(count - 1)]
        down = [(j, i) for i, j in up]
        last = lax.slice_in_dim(x, length - width, length, axis=dim)
        first = lax.slice_in_dim(x, 0, width, axis=dim)
        before = lax.ppermute(last, axis, up)
        after = lax.ppermute(first, axis, down)
        x = jnp.concatenate([before, x, after], axis=dim)
    return x


def rock_rate(classes):
    result = rock_rates[0] * (classes == 0).astype(jnp.float32)
    for klass in range(1, 4):
        result = result + rock_rates[klass] * (classes == klass).astype(jnp.float32)
    return result


def talus_flow(diff):
    return (
        jax.nn.softplus(talus_sharp * (diff - talus_drop))
        - jax.nn.softplus(talus_sharp * (-diff - talus_drop))
    ) / talus_sharp


def advance(padded, erod, row_ok, col_ok):
    rows_out = padded.shape[1] - 4
    cols_out = padded.shape[2] - 4

    def inner(field, row_step, col_step):
        return field[
            ..., 1 + row_step : 3 + row_step + rows_out, 1 + col_step : 3 + col_step + cols_out
        ]

    def middle(field, row_step, col_step):
        return field[1 + row_step : 1 + row_step + rows_out, 1 + col_step : 1 + col_step + cols_out]

    def core(field, row_step, col_step):
        return field[
            ..., 2 + row_step : 2 + row_step + rows_out, 2 + col_step : 2 + col_step + cols_out
        ]

    height = padded[0]
    water_now = padded[1]
    surface = height + water_now
    inside = row_ok[1 : 3 + rows_out][:, None] * col_ok[1 : 3 + cols_out][None, :]
    left_ok = col_ok[0 : 2 + cols_out][None, :]
    right_ok = col_ok[2 : 4 + cols_out][None, :]
    upper_ok = row_ok[0 : 2 + rows_out][:, None]
    lower_ok = row_ok[2 : 4 + rows_out][:, None]
    centre = inner(surface, 0, 0)
    to_left = (
        jnp.maximum(0.0, inner(padded[3], 0, 0) + time_step * (centre - inner(surface, 0, -1)))
        * left_ok
        * inside
    )
    to_right = (
        jnp.maximum(0.0, inner(padded[4], 0, 0) + time_step * (centre - inner(surface, 0, 1)))
        * right_ok
        * inside
    )
    to_upper = (
        jnp.maximum(0.0, inner(padded[5], 0, 0) + time_step * (centre - inner(surface, -1, 0)))
        * upper_ok
        * inside
    )
    to_lower = (
        jnp.maximum(0.0, inner(padded[6], 0, 0) + time_step * (centre - inner(surface, 1, 0)))
        * lower_ok
        * inside
    )
    raw_total = to_left + to_right + to_upper + to_lower
    limiter = jnp.minimum(
        1.0, inner(water_now, 0, 0) / jnp.maximum(time_step * raw_total, wet_floor)
    )
    to_left = to_left * limiter
    to_right = to_right * limiter
    to_upper = to_upper * limiter
    to_lower = to_lower * limiter
    carried = inner(padded[2], 0, 0) / jnp.maximum(inner(water_now, 0, 0), deep_floor)
    outflow = (
        middle(to_left, 0, 0)
        + middle(to_right, 0, 0)
        + middle(to_upper, 0, 0)
        + middle(to_lower, 0, 0)
    )
    inflow = (
        middle(to_right, 0, -1)
        + middle(to_left, 0, 1)
        + middle(to_lower, -1, 0)
        + middle(to_upper, 1, 0)
    )
    water_old = core(water_now, 0, 0)
    water_new = water_old + time_step * (inflow - outflow)
    across = 0.5 * (
        middle(to_right, 0, -1)
        - middle(to_left, 0, 0)
        + middle(to_right, 0, 0)
        - middle(to_left, 0, 1)
    )
    along = 0.5 * (
        middle(to_lower, -1, 0)
        - middle(to_upper, 0, 0)
        + middle(to_lower, 0, 0)
        - middle(to_upper, 1, 0)
    )
    mean_depth = jnp.maximum(0.5 * (water_old + water_new), deep_floor)
    speed_u = padded[7]
    speed_v = padded[8]
    smooth_u = (
        4.0 * core(speed_u, 0, 0)
        + core(speed_u, 0, -1)
        + core(speed_u, 0, 1)
        + core(speed_u, -1, 0)
        + core(speed_u, 1, 0)
    ) / 16.0
    smooth_v = (
        4.0 * core(speed_v, 0, 0)
        + core(speed_v, 0, -1)
        + core(speed_v, 0, 1)
        + core(speed_v, -1, 0)
        + core(speed_v, 1, 0)
    ) / 16.0
    new_u = across / (2.0 * mean_depth) + smooth_u
    new_v = along / (2.0 * mean_depth) + smooth_v
    sediment = core(padded[2], 0, 0) + time_step * (
        middle(to_right, 0, -1) * middle(carried, 0, -1)
        + middle(to_left, 0, 1) * middle(carried, 0, 1)
        + middle(to_lower, -1, 0) * middle(carried, -1, 0)
        + middle(to_upper, 1, 0) * middle(carried, 1, 0)
        - outflow * middle(carried, 0, 0)
    )
    left_in = col_ok[1 : 1 + cols_out][None, :]
    right_in = col_ok[3 : 3 + cols_out][None, :]
    upper_in = row_ok[1 : 1 + rows_out][:, None]
    lower_in = row_ok[3 : 3 + rows_out][:, None]
    base = core(height, 0, 0)
    diff_left = core(height, 0, -1) - base
    diff_right = core(height, 0, 1) - base
    diff_upper = core(height, -1, 0) - base
    diff_lower = core(height, 1, 0) - base
    grad_x = 0.5 * (right_in * diff_right - left_in * diff_left)
    grad_y = 0.5 * (lower_in * diff_lower - upper_in * diff_upper)
    grad_sq = grad_x * grad_x + grad_y * grad_y
    capacity = carry_coef * jnp.sqrt(
        (new_u * new_u + new_v * new_v) * grad_sq / (1.0 + grad_sq) + cap_floor
    )
    gap_left = capacity - sediment
    delta = jnp.where(gap_left > 0.0, erode_coef * erod * gap_left, settle_coef * gap_left)
    thermal = slide_coef * (
        left_in * talus_flow(diff_left)
        + right_in * talus_flow(diff_right)
        + upper_in * talus_flow(diff_upper)
        + lower_in * talus_flow(diff_lower)
    )
    new_height = base - delta + thermal
    new_sediment = sediment + delta
    out_ok = row_ok[2 : 2 + rows_out][:, None] * col_ok[2 : 2 + cols_out][None, :]
    fresh = jnp.stack(
        [
            new_height,
            water_new,
            new_sediment,
            middle(to_left, 0, 0),
            middle(to_right, 0, 0),
            middle(to_upper, 0, 0),
            middle(to_lower, 0, 0),
            new_u,
            new_v,
        ]
    )
    return fresh * out_ok[None]


def settle(fresh, rain_field, mean_water):
    return fresh.at[1].set(fresh[1] * (1.0 - evap_coef * mean_water) + rain_depth * rain_field)


def valid_line(index, extent, whole, margin):
    places = index * extent + jnp.arange(-margin, extent + margin, dtype=jnp.int32)
    return ((places >= 0) & (places < whole)).astype(jnp.float32)


def extend(field, width):
    return with_halo(field, (("rows", 1), ("cols", 2)), width)


def square_mean(own_water, cells):
    return lax.psum(jnp.sum(own_water * own_water), ("rows", "cols")) / cells


def shards(state, hardness, rain_mask):
    rows_own = state.shape[1]
    cols_own = state.shape[2]
    whole_rows = rows_own * lax.axis_size("rows")
    whole_cols = cols_own * lax.axis_size("cols")
    cells = float(whole_rows * whole_cols)
    row_index = lax.axis_index("rows")
    col_index = lax.axis_index("cols")
    erod_own = rock_rate(hardness)
    rain_own = rain_mask.astype(jnp.float32)
    row_ok = valid_line(row_index, rows_own, whole_rows, 2)
    col_ok = valid_line(col_index, cols_own, whole_cols, 2)
    for step in range(STEPS):
        padded = extend(state, 2)
        fresh = advance(padded, erod_own, row_ok, col_ok)
        mean_water = square_mean(fresh[1], cells)
        state = settle(fresh, rain_own, mean_water)
    return state


def solution(mesh):
    in_specs = (P(None, "rows", "cols"), P("rows", "cols"), P("rows", "cols"))
    out_specs = P(None, "rows", "cols")
    return jax.shard_map(shards, mesh=mesh, in_specs=in_specs, out_specs=out_specs, check_vma=False)
```

profile of v0, /device:TPU:24, one launch (start us, length us, event | category | flops | bytes accessed | tf_op | source)
XLA Modules:
  0.0 926.0 jit_solution(3838931543471333639)
XLA Ops:
  1.0 3.6 collective-permute-start
  7.3 5.3 collective-permute-done.1
  16.4 5.4 collective-permute-done.3
  34.0 83.4 %psum.56 = f32[]{:T(128)} all-reduce(f32[]{:T(128)} %get-tuple-element.305), channel_id=1, replica_groups=mesh['rows'=32,'cols'=8] {'rows','cols'}, use_global_device_ids=true, to_apply=%region_1.2 | all-reduce | flops 1 | bytes 8 | tf_op jit(solution)/shard_map/psum | solution.py:214
  119.6 3.3 collective-permute-start.4
  125.5 5.4 collective-permute-done.5
  134.6 3.6 collective-permute-done.7
  150.6 82.2 %psum.57 = f32[]{:T(128)} all-reduce(f32[]{:T(128)} %get-tuple-element.301), channel_id=1, replica_groups=mesh['rows'=32,'cols'=8] {'rows','cols'}, use_global_device_ids=true, to_apply=%region_3.4 | all-reduce | flops 1 | bytes 8 | tf_op jit(solution)/shard_map/psum | solution.py:214
  237.4 3.5 collective-permute-start.9
  240.9 4.4 collective-permute-done.9
  249.1 3.7 collective-permute-done.11
  265.2 83.0 %psum.58 = f32[]{:T(128)} all-reduce(f32[]{:T(128)} %get-tuple-element.297), channel_id=1, replica_groups=mesh['rows'=32,'cols'=8] {'rows','cols'}, use_global_device_ids=true, to_apply=%region_5.6 | all-reduce | flops 1 | bytes 8 | tf_op jit(solution)/shard_map/psum | solution.py:214
  350.4 3.1 collective-permute-start.12
  356.3 5.2 collective-permute-done.13
  365.4 3.5 collective-permute-done.15
  381.3 82.2 %psum.59 = f32[]{:T(128)} all-reduce(f32[]{:T(128)} %get-tuple-element.293), channel_id=1, replica_groups=mesh['rows'=32,'cols'=8] {'rows','cols'}, use_global_device_ids=true, to_apply=%region_7.8 | all-reduce | flops 1 | bytes 8 | tf_op jit(solution)/shard_map/psum | solution.py:214
  465.7 3.1 collective-permute-start.16
  471.6 5.2 collective-permute-done.17
  480.6 3.7 collective-permute-done.19
  496.6 82.2 %psum.60 = f32[]{:T(128)} all-reduce(f32[]{:T(128)} %get-tuple-element.289), channel_id=1, replica_groups=mesh['rows'=32,'cols'=8] {'rows','cols'}, use_global_device_ids=true, to_apply=%region_9.10 | all-reduce | flops 1 | bytes 8 | tf_op jit(solution)/shard_map/psum | solution.py:214
  581.1 3.1 collective-permute-start.20
  586.9 5.2 collective-permute-done.21
  595.9 3.7 collective-permute-done.23
  612.0 82.2 %psum.61 = f32[]{:T(128)} all-reduce(f32[]{:T(128)} %get-tuple-element.285), channel_id=1, replica_groups=mesh['rows'=32,'cols'=8] {'rows','cols'}, use_global_device_ids=true, to_apply=%region_11.12 | all-reduce | flops 1 | bytes 8 | tf_op jit(solution)/shard_map/psum | solution.py:214
  696.4 3.1 collective-permute-start.24
  702.3 5.2 collective-permute-done.25
  711.5 3.5 collective-permute-done.27
  727.3 82.2 %psum.62 = f32[]{:T(128)} all-reduce(f32[]{:T(128)} %get-tuple-element.281), channel_id=1, replica_groups=mesh['rows'=32,'cols'=8] {'rows','cols'}, use_global_device_ids=true, to_apply=%region_13.14 | all-reduce | flops 1 | bytes 8 | tf_op jit(solution)/shard_map/psum | solution.py:214
  811.7 3.1 collective-permute-start.28
  817.6 5.2 collective-permute-done.29
  826.6 3.7 collective-permute-done.31
  842.6 82.2 %psum.63 = f32[]{:T(128)} all-reduce(f32[]{:T(128)} %get-tuple-element.277), channel_id=1, replica_groups=mesh['rows'=32,'cols'=8] {'rows','cols'}, use_global_device_ids=true, to_apply=%region_15.16 | all-reduce | flops 1 | bytes 8 | tf_op jit(solution)/shard_map/psum | solution.py:214
  (205 shorter events, 163.0 us)
Async XLA Ops:
  1.0 6.3 collective-permute-start
  4.7 8.0 collective-permute-start.1
  13.7 2.7 collective-permute-start.2
  15.0 6.8 collective-permute-start.3
  119.6 5.9 collective-permute-start.4
  122.9 8.0 collective-permute-start.5
  132.0 2.6 collective-permute-start.6
  133.3 5.0 collective-permute-start.7
  235.1 5.9 collective-permute-start.8
  237.4 8.0 collective-permute-start.9
  246.5 2.6 collective-permute-start.10
  247.8 5.0 collective-permute-start.11
  350.4 5.9 collective-permute-start.12
  353.5 8.0 collective-permute-start.13
  362.6 2.8 collective-permute-start.14
  363.9 5.0 collective-permute-start.15
  465.7 5.9 collective-permute-start.16
  468.9 8.0 collective-permute-start.17
  478.0 2.6 collective-permute-start.18
  479.3 5.0 collective-permute-start.19
  581.1 5.9 collective-permute-start.20
  584.2 8.0 collective-permute-start.21
  593.3 2.6 collective-permute-start.22
  594.6 5.0 collective-permute-start.23
  696.4 5.9 collective-permute-start.24
  699.5 8.0 collective-permute-start.25
  708.6 2.8 collective-permute-start.26
  709.9 5.0 collective-permute-start.27
  811.7 5.9 collective-permute-start.28
  814.9 8.0 collective-permute-start.29
  824.0 2.6 collective-permute-start.30
  825.3 5.0 collective-permute-start.31
  (3 other events, 107.2 us)
where the time goes:
time: 930 us; the launch traced here: 926 us
  blocking collectives  660 us (71%)
  other arithmetic  73.4 us (8%)
  waiting for transfers between devices  72.2 us (8%)
  starting transfers between devices  68 us (7%)
  local copies, waits for them, and re-layouts  47.6 us (5%)
    psum x8, blocking collectives, square_mean(): return lax.psum(jnp.sum(own_water * own_water), ('rows', 'cols')) / cells  660 us
    ppermute x16, waiting for transfers between devices, with_halo(): after = lax.ppermute(first, axis, down)  72.1 us
    ppermute x16, starting transfers between devices, with_halo(): before = lax.ppermute(last, axis, up)  35.3 us
    unnamed x54, local copies, waits for them, and re-layouts  33.8 us
    ppermute x16, starting transfers between devices, with_halo(): after = lax.ppermute(first, axis, down)  32.7 us
  transfers between devices with their start and end apart: 32, of which 16 were waited for; matrix products, arithmetic and copies ran while one was open for 0% of the time, Pallas kernels for 0%

commit v1 on v0

--- a/solution.py
+++ b/solution.py
@@ -206,12 +206,16 @@
     return ((places >= 0) & (places < whole)).astype(jnp.float32)
 
 
-def extend(field, width):
-    return with_halo(field, (("rows", 1), ("cols", 2)), width)
-
-
-def square_mean(own_water, cells):
-    return lax.psum(jnp.sum(own_water * own_water), ("rows", "cols")) / cells
+def butterfly_sum(value):
+    total = jnp.broadcast_to(value, (1, 128))
+    for axis in ("cols", "rows"):
+        count = lax.axis_size(axis)
+        bit = 1
+        while bit < count:
+            pairs = [(i, i ^ bit) for i in range(count)]
+            total = total + lax.ppermute(total, axis, pairs)
+            bit *= 2
+    return total[0, 0]
 
 
 def shards(state, hardness, rain_mask):
@@ -224,14 +228,30 @@
     col_index = lax.axis_index("cols")
     erod_own = rock_rate(hardness)
     rain_own = rain_mask.astype(jnp.float32)
-    row_ok = valid_line(row_index, rows_own, whole_rows, 2)
-    col_ok = valid_line(col_index, cols_own, whole_cols, 2)
+    width = 2 * STEPS
+    stacked = jnp.concatenate([state, erod_own[None], rain_own[None]], axis=0)
+    stacked = with_halo(stacked, (("rows", 1), ("cols", 2)), width)
+    current = stacked[:9]
+    erod_ext = stacked[9]
+    rain_ext = stacked[10]
+    row_ok = valid_line(row_index, rows_own, whole_rows, width)
+    col_ok = valid_line(col_index, cols_own, whole_cols, width)
     for step in range(STEPS):
-        padded = extend(state, 2)
-        fresh = advance(padded, erod_own, row_ok, col_ok)
-        mean_water = square_mean(fresh[1], cells)
-        state = settle(fresh, rain_own, mean_water)
-    return state
+        margin = width - 2 * step
+        cut = 2 * step
+        row_ok_now = row_ok[cut : cut + rows_own + 2 * margin]
+        col_ok_now = col_ok[cut : cut + cols_own + 2 * margin]
+        inner_cut = cut + 2
+        out_rows = rows_own + 2 * margin - 4
+        out_cols = cols_own + 2 * margin - 4
+        erod_now = erod_ext[inner_cut : inner_cut + out_rows, inner_cut : inner_cut + out_cols]
+        rain_now = rain_ext[inner_cut : inner_cut + out_rows, inner_cut : inner_cut + out_cols]
+        fresh = advance(current, erod_now, row_ok_now, col_ok_now)
+        keep = margin - 2
+        own_water = fresh[1, keep : keep + rows_own, keep : keep + cols_own]
+        mean_water = butterfly_sum(jnp.sum(own_water * own_water)) / cells
+        current = settle(fresh, rain_now, mean_water)
+    return current
 
 
 def solution(mesh):

time: 930 us -> 367 us (0.39)
  blocking collectives: 660 us -> 0 us
  waiting for transfers between devices: 72.2 us -> 198 us
  starting transfers between devices: 68 us -> 111 us
  local copies, waits for them, and re-layouts: 47.6 us -> 10.3 us
  other arithmetic: 73.4 us -> 39.2 us
    psum x8 -> x0, blocking collectives: 660 us -> none  [square_mean(): return lax.psum(jnp.sum(own_water * own_water), ('rows', 'cols')) / cells]
    ppermute x0 -> x64, waiting for transfers between devices: none -> 181 us  [butterfly_sum(): total = total + lax.ppermute(total, axis, pairs)]
    ppermute x0 -> x64, starting transfers between devices: none -> 103 us  [butterfly_sum(): total = total + lax.ppermute(total, axis, pairs)]
    ppermute x16 -> x2, waiting for transfers between devices: 72.1 us -> 11 us  [with_halo(): after = lax.ppermute(first, axis, down)]
    unnamed x54 -> x52, local copies, waits for them, and re-layouts: 33.8 us -> 3.25 us
    ppermute x16 -> x2, starting transfers between devices: 35.3 us -> 4.8 us  [with_halo(): before = lax.ppermute(last, axis, up)]
    ppermute x16 -> x2, starting transfers between devices: 32.7 us -> 3.65 us  [with_halo(): after = lax.ppermute(first, axis, down)]
    mul x8, other arithmetic: 15.5 us -> 0.68 us  [advance(): return fresh * out_ok[None]]
  transfers between devices with their start and end apart: 32 -> 68, of which waited for: 16 -> 67; matrix products, arithmetic and copies ran while one was open for 0% -> 1% of each run, Pallas kernels for 0% -> 0%
where the time goes in v1:
time: 367 us; the launch traced here: 360 us
  waiting for transfers between devices  198 us (54%)
  starting transfers between devices  111 us (30%)
  other arithmetic  39.2 us (11%)
  local copies, waits for them, and re-layouts  10.3 us (3%)
    ppermute x64, waiting for transfers between devices, butterfly_sum(): total = total + lax.ppermute(total, axis, pairs)  181 us
    ppermute x64, starting transfers between devices, butterfly_sum(): total = total + lax.ppermute(total, axis, pairs)  103 us
    unnamed x16, other arithmetic  11.4 us
    ppermute x2, waiting for transfers between devices, with_halo(): after = lax.ppermute(first, axis, down)  11 us
    add x64, other arithmetic, butterfly_sum(): total = total + lax.ppermute(total, axis, pairs)  10.5 us
  transfers between devices with their start and end apart: 68, of which 67 were waited for; matrix products, arithmetic and copies ran while one was open for 1% of the time, Pallas kernels for 0%

profile of v1, /device:TPU:24, one launch (start us, length us, event | category | flops | bytes accessed | tf_op | source)
XLA Modules:
  0.0 360.2 jit_solution(7778541190255812279)
XLA Ops:
  3.0 3.5 collective-permute-start
  9.2 5.8 %collective-permute-done = f32[11,16,512]{2,1,0:T(8,128)S(1)} collective-permute-done((f32[11,16,512]{2,1,0:T(8,128)S(1)}, f32[11,16,512]{2,1,0:T(8,128)S(1)}, u32[]{:S(2)}, u32[]{:S(2)}) %collective-permute-start) | collective-permute-done | bytes 360480 | tf_op jit(solution)/shard_map/ppermute | solution.py:31
  15.0 5.3 %collective-permute-done.1 = f32[11,16,512]{2,1,0:T(8,128)S(1)} collective-permute-done((f32[11,16,512]{2,1,0:T(8,128)S(1)}, f32[11,16,512]{2,1,0:T(8,128)S(1)}, u32[]{:S(2)}, u32[]{:S(2)}) %collective-permute-start.1) | collective-permute-done | bytes 360480 | tf_op jit(solution)/shard_map/ppermute | solution.py:32
  23.2 5.7 %collective-permute-done.3 = f32[11,64,16]{2,1,0:T(8,128)S(1)} collective-permute-done((f32[11,64,16]{2,1,0:T(8,128)S(1)}, f32[11,64,16]{2,1,0:T(8,128)S(1)}, u32[]{:S(2)}, u32[]{:S(2)}) %collective-permute-start.3) | collective-permute-done | bytes 45088 | tf_op jit(solution)/shard_map/ppermute | solution.py:32
  34.3 10.5 %collective-permute-start.4 = (f32[1,128]{1,0:T(1,128)S(1)}, f32[1,128]{1,0:T(1,128)S(1)}, u32[]{:S(2)}, u32[]{:S(2)}) collective-permute-start(f32[1,128]{1,0:T(1,128)S(1)} %broadcast_in_dim.22), channel_id=1, source_target_pairs={{0,1},{1,0},{2,3},{3,2},{4,5},{5,4},{6,7},{7,6},{8,9},{9,8},{10,11... | collective-permute-start | bytes 1544 | tf_op jit(solution)/shard_map/ppermute | solution.py:216
  46.3 4.8 %collective-permute-start.5 = (f32[1,128]{1,0:T(1,128)S(1)}, f32[1,128]{1,0:T(1,128)S(1)}, u32[]{:S(2)}, u32[]{:S(2)}) collective-permute-start(f32[1,128]{1,0:T(1,128)S(1)} %broadcast_add_fusion.7), channel_id=1, source_target_pairs={{0,2},{1,3},{2,0},{3,1},{4,6},{5,7},{6,4},{7,5},{8,10},{9,11},{10,... | collective-permute-start | bytes 1544 | tf_op jit(solution)/shard_map/ppermute | solution.py:216
  56.2 4.6 %collective-permute-done.6 = f32[1,128]{1,0:T(1,128)S(1)} collective-permute-done((f32[1,128]{1,0:T(1,128)S(1)}, f32[1,128]{1,0:T(1,128)S(1)}, u32[]{:S(2)}, u32[]{:S(2)}) %collective-permute-start.6) | collective-permute-done | bytes 544 | tf_op jit(solution)/shard_map/ppermute | solution.py:216
  60.9 3.5 collective-permute-done.7
  64.5 5.0 %collective-permute-done.8 = f32[1,128]{1,0:T(1,128)S(1)} collective-permute-done((f32[1,128]{1,0:T(1,128)S(1)}, f32[1,128]{1,0:T(1,128)S(1)}, u32[]{:S(2)}, u32[]{:S(2)}) %collective-permute-start.8) | collective-permute-done | bytes 544 | tf_op jit(solution)/shard_map/ppermute | solution.py:216
  76.6 3.4 collective-permute-start.11
  96.7 4.6 %collective-permute-done.14 = f32[1,128]{1,0:T(1,128)S(1)} collective-permute-done((f32[1,128]{1,0:T(1,128)S(1)}, f32[1,128]{1,0:T(1,128)S(1)}, u32[]{:S(2)}, u32[]{:S(2)}) %collective-permute-start.14) | collective-permute-done | bytes 544 | tf_op jit(solution)/shard_map/ppermute | solution.py:216
  101.3 3.5 collective-permute-done.15
  104.9 5.0 %collective-permute-done.16 = f32[1,128]{1,0:T(1,128)S(1)} collective-permute-done((f32[1,128]{1,0:T(1,128)S(1)}, f32[1,128]{1,0:T(1,128)S(1)}, u32[]{:S(2)}, u32[]{:S(2)}) %collective-permute-start.16) | collective-permute-done | bytes 544 | tf_op jit(solution)/shard_map/ppermute | solution.py:216
  136.7 4.6 %collective-permute-done.22 = f32[1,128]{1,0:T(1,128)S(1)} collective-permute-done((f32[1,128]{1,0:T(1,128)S(1)}, f32[1,128]{1,0:T(1,128)S(1)}, u32[]{:S(2)}, u32[]{:S(2)}) %collective-permute-start.22) | collective-permute-done | bytes 544 | tf_op jit(solution)/shard_map/ppermute | solution.py:216
  141.4 3.5 collective-permute-done.23
  145.0 5.0 %collective-permute-done.24 = f32[1,128]{1,0:T(1,128)S(1)} collective-permute-done((f32[1,128]{1,0:T(1,128)S(1)}, f32[1,128]{1,0:T(1,128)S(1)}, u32[]{:S(2)}, u32[]{:S(2)}) %collective-permute-start.24) | collective-permute-done | bytes 544 | tf_op jit(solution)/shard_map/ppermute | solution.py:216
  176.4 4.6 %collective-permute-done.30 = f32[1,128]{1,0:T(1,128)S(1)} collective-permute-done((f32[1,128]{1,0:T(1,128)S(1)}, f32[1,128]{1,0:T(1,128)S(1)}, u32[]{:S(2)}, u32[]{:S(2)}) %collective-permute-start.30) | collective-permute-done | bytes 544 | tf_op jit(solution)/shard_map/ppermute | solution.py:216
  181.1 3.5 collective-permute-done.31
  184.6 5.0 %collective-permute-done.32 = f32[1,128]{1,0:T(1,128)S(1)} collective-permute-done((f32[1,128]{1,0:T(1,128)S(1)}, f32[1,128]{1,0:T(1,128)S(1)}, u32[]{:S(2)}, u32[]{:S(2)}) %collective-permute-start.32) | collective-permute-done | bytes 544 | tf_op jit(solution)/shard_map/ppermute | solution.py:216
  196.8 3.4 collective-permute-start.35
  216.3 4.6 %collective-permute-done.38 = f32[1,128]{1,0:T(1,128)S(1)} collective-permute-done((f32[1,128]{1,0:T(1,128)S(1)}, f32[1,128]{1,0:T(1,128)S(1)}, u32[]{:S(2)}, u32[]{:S(2)}) %collective-permute-start.38) | collective-permute-done | bytes 544 | tf_op jit(solution)/shard_map/ppermute | solution.py:216
  221.0 3.5 collective-permute-done.39
  224.6 5.0 %collective-permute-done.40 = f32[1,128]{1,0:T(1,128)S(1)} collective-permute-done((f32[1,128]{1,0:T(1,128)S(1)}, f32[1,128]{1,0:T(1,128)S(1)}, u32[]{:S(2)}, u32[]{:S(2)}) %collective-permute-start.40) | collective-permute-done | bytes 544 | tf_op jit(solution)/shard_map/ppermute | solution.py:216
  255.6 4.6 %collective-permute-done.46 = f32[1,128]{1,0:T(1,128)S(1)} collective-permute-done((f32[1,128]{1,0:T(1,128)S(1)}, f32[1,128]{1,0:T(1,128)S(1)}, u32[]{:S(2)}, u32[]{:S(2)}) %collective-permute-start.46) | collective-permute-done | bytes 544 | tf_op jit(solution)/shard_map/ppermute | solution.py:216
  260.3 3.5 collective-permute-done.47
  263.9 5.0 %collective-permute-done.48 = f32[1,128]{1,0:T(1,128)S(1)} collective-permute-done((f32[1,128]{1,0:T(1,128)S(1)}, f32[1,128]{1,0:T(1,128)S(1)}, u32[]{:S(2)}, u32[]{:S(2)}) %collective-permute-start.48) | collective-permute-done | bytes 544 | tf_op jit(solution)/shard_map/ppermute | solution.py:216
  295.1 4.5 %collective-permute-done.54 = f32[1,128]{1,0:T(1,128)S(1)} collective-permute-done((f32[1,128]{1,0:T(1,128)S(1)}, f32[1,128]{1,0:T(1,128)S(1)}, u32[]{:S(2)}, u32[]{:S(2)}) %collective-permute-start.54) | collective-permute-done | bytes 544 | tf_op jit(solution)/shard_map/ppermute | solution.py:216
  299.7 3.5 collective-permute-done.55
  303.3 5.0 %collective-permute-done.56 = f32[1,128]{1,0:T(1,128)S(1)} collective-permute-done((f32[1,128]{1,0:T(1,128)S(1)}, f32[1,128]{1,0:T(1,128)S(1)}, u32[]{:S(2)}, u32[]{:S(2)}) %collective-permute-start.56) | collective-permute-done | bytes 544 | tf_op jit(solution)/shard_map/ppermute | solution.py:216
  333.8 4.6 %collective-permute-done.62 = f32[1,128]{1,0:T(1,128)S(1)} collective-permute-done((f32[1,128]{1,0:T(1,128)S(1)}, f32[1,128]{1,0:T(1,128)S(1)}, u32[]{:S(2)}, u32[]{:S(2)}) %collective-permute-start.62) | collective-permute-done | bytes 544 | tf_op jit(solution)/shard_map/ppermute | solution.py:216
  338.4 3.6 collective-permute-done.63
  342.0 5.1 %collective-permute-done.64 = f32[1,128]{1,0:T(1,128)S(1)} collective-permute-done((f32[1,128]{1,0:T(1,128)S(1)}, f32[1,128]{1,0:T(1,128)S(1)}, u32[]{:S(2)}, u32[]{:S(2)}) %collective-permute-start.64) | collective-permute-done | bytes 544 | tf_op jit(solution)/shard_map/ppermute | solution.py:216
  (349 shorter events, 211.3 us)
Async XLA Ops:
  3.0 12.0 %collective-permute-start = (f32[11,16,512]{2,1,0:T(8,128)S(1)}, f32[11,16,512]{2,1,0:T(8,128)S(1)}, u32[]{:S(2)}, u32[]{:S(2)}) collective-permute-start(f32[11,16,512]{2,1,0:T(8,128)S(1)} %get-tuple-element.272), channel_id=1, source_target_pairs={{0,8},{8,16},{16,24},{24,32},{32,40},{40,48},{48,56},{56,64},{64,7... | collective-permute-start | bytes 1081352 | tf_op jit(solution)/shard_map/ppermute | solution.py:31
  6.5 13.9 %collective-permute-start.1 = (f32[11,16,512]{2,1,0:T(8,128)S(1)}, f32[11,16,512]{2,1,0:T(8,128)S(1)}, u32[]{:S(2)}, u32[]{:S(2)}) collective-permute-start(f32[11,16,512]{2,1,0:T(8,128)S(1)} %get-tuple-element.273), channel_id=1, source_target_pairs={{8,0},{16,8},{24,16},{32,24},{40,32},{48,40},{56,48},{64,56},{72,6... | collective-permute-start | bytes 1081352 | tf_op jit(solution)/shard_map/ppermute | solution.py:32
  21.9 7.1 %collective-permute-start.3 = (f32[11,64,16]{2,1,0:T(8,128)S(1)}, f32[11,64,16]{2,1,0:T(8,128)S(1)}, u32[]{:S(2)}, u32[]{:S(2)}) collective-permute-start(f32[11,64,16]{2,1,0:T(8,128)S(1)} %get-tuple-element.223), channel_id=1, source_target_pairs={{1,0},{2,1},{3,2},{4,3},{5,4},{6,5},{7,6},{9,8},{10,9},{11,10},{12... | collective-permute-start | bytes 135176 | tf_op jit(solution)/shard_map/ppermute | solution.py:32
  34.3 11.3 %collective-permute-start.4 = (f32[1,128]{1,0:T(1,128)S(1)}, f32[1,128]{1,0:T(1,128)S(1)}, u32[]{:S(2)}, u32[]{:S(2)}) collective-permute-start(f32[1,128]{1,0:T(1,128)S(1)} %broadcast_in_dim.22), channel_id=1, source_target_pairs={{0,1},{1,0},{2,3},{3,2},{4,5},{5,4},{6,7},{7,6},{8,9},{9,8},{10,11... | collective-permute-start | bytes 1544 | tf_op jit(solution)/shard_map/ppermute | solution.py:216
  46.3 6.3 %collective-permute-start.5 = (f32[1,128]{1,0:T(1,128)S(1)}, f32[1,128]{1,0:T(1,128)S(1)}, u32[]{:S(2)}, u32[]{:S(2)}) collective-permute-start(f32[1,128]{1,0:T(1,128)S(1)} %broadcast_add_fusion.7), channel_id=1, source_target_pairs={{0,2},{1,3},{2,0},{3,1},{4,6},{5,7},{6,4},{7,5},{8,10},{9,11},{10,... | collective-permute-start | bytes 1544 | tf_op jit(solution)/shard_map/ppermute | solution.py:216
  53.3 7.6 %collective-permute-start.6 = (f32[1,128]{1,0:T(1,128)S(1)}, f32[1,128]{1,0:T(1,128)S(1)}, u32[]{:S(2)}, u32[]{:S(2)}) collective-permute-start(f32[1,128]{1,0:T(1,128)S(1)} %fusion.468), channel_id=1, source_target_pairs={{0,4},{1,5},{2,6},{3,7},{4,0},{5,1},{6,2},{7,3},{8,12},{9,13},{10,... | collective-permute-start | bytes 1544 | tf_op jit(solution)/shard_map/ppermute | solution.py:216
  64.4 5.1 %collective-permute-start.8 = (f32[1,128]{1,0:T(1,128)S(1)}, f32[1,128]{1,0:T(1,128)S(1)}, u32[]{:S(2)}, u32[]{:S(2)}) collective-permute-start(f32[1,128]{1,0:T(1,128)S(1)} %add.1626), channel_id=1, source_target_pairs={{0,16},{8,24},{16,0},{24,8},{32,48},{40,56},{48,32},{56,40},{64,80... | collective-permute-start | bytes 1544 | tf_op jit(solution)/shard_map/ppermute | solution.py:216
  76.6 5.5 %collective-permute-start.11 = (f32[1,128]{1,0:T(1,128)S(1)}, f32[1,128]{1,0:T(1,128)S(1)}, u32[]{:S(2)}, u32[]{:S(2)}) collective-permute-start(f32[1,128]{1,0:T(1,128)S(1)} %add.1629), channel_id=1, source_target_pairs={{0,128},{8,136},{16,144},{24,152},{32,160},{40,168},{48,176},{56,1... | collective-permute-start | bytes 1544 | tf_op jit(solution)/shard_map/ppermute | solution.py:216
  88.5 4.6 %collective-permute-start.13 = (f32[1,128]{1,0:T(1,128)S(1)}, f32[1,128]{1,0:T(1,128)S(1)}, u32[]{:S(2)}, u32[]{:S(2)}) collective-permute-start(f32[1,128]{1,0:T(1,128)S(1)} %broadcast_add_fusion.6), channel_id=1, source_target_pairs={{0,2},{1,3},{2,0},{3,1},{4,6},{5,7},{6,4},{7,5},{8,10},{9,11},{10,... | collective-permute-start | bytes 1544 | tf_op jit(solution)/shard_map/ppermute | solution.py:216
  93.7 7.6 %collective-permute-start.14 = (f32[1,128]{1,0:T(1,128)S(1)}, f32[1,128]{1,0:T(1,128)S(1)}, u32[]{:S(2)}, u32[]{:S(2)}) collective-permute-start(f32[1,128]{1,0:T(1,128)S(1)} %fusion.467), channel_id=1, source_target_pairs={{0,4},{1,5},{2,6},{3,7},{4,0},{5,1},{6,2},{7,3},{8,12},{9,13},{10,... | collective-permute-start | bytes 1544 | tf_op jit(solution)/shard_map/ppermute | solution.py:216
  104.8 5.1 %collective-permute-start.16 = (f32[1,128]{1,0:T(1,128)S(1)}, f32[1,128]{1,0:T(1,128)S(1)}, u32[]{:S(2)}, u32[]{:S(2)}) collective-permute-start(f32[1,128]{1,0:T(1,128)S(1)} %add.1686), channel_id=1, source_target_pairs={{0,16},{8,24},{16,0},{24,8},{32,48},{40,56},{48,32},{56,40},{64,80... | collective-permute-start | bytes 1544 | tf_op jit(solution)/shard_map/ppermute | solution.py:216
  117.1 5.1 %collective-permute-start.19 = (f32[1,128]{1,0:T(1,128)S(1)}, f32[1,128]{1,0:T(1,128)S(1)}, u32[]{:S(2)}, u32[]{:S(2)}) collective-permute-start(f32[1,128]{1,0:T(1,128)S(1)} %add.1689), channel_id=1, source_target_pairs={{0,128},{8,136},{16,144},{24,152},{32,160},{40,168},{48,176},{56,1... | collective-permute-start | bytes 1544 | tf_op jit(solution)/shard_map/ppermute | solution.py:216
  133.6 7.7 %collective-permute-start.22 = (f32[1,128]{1,0:T(1,128)S(1)}, f32[1,128]{1,0:T(1,128)S(1)}, u32[]{:S(2)}, u32[]{:S(2)}) collective-permute-start(f32[1,128]{1,0:T(1,128)S(1)} %fusion.466), channel_id=1, source_target_pairs={{0,4},{1,5},{2,6},{3,7},{4,0},{5,1},{6,2},{7,3},{8,12},{9,13},{10,... | collective-permute-start | bytes 1544 | tf_op jit(solution)/shard_map/ppermute | solution.py:216
  144.9 5.1 %collective-permute-start.24 = (f32[1,128]{1,0:T(1,128)S(1)}, f32[1,128]{1,0:T(1,128)S(1)}, u32[]{:S(2)}, u32[]{:S(2)}) collective-permute-start(f32[1,128]{1,0:T(1,128)S(1)} %add.1746), channel_id=1, source_target_pairs={{0,16},{8,24},{16,0},{24,8},{32,48},{40,56},{48,32},{56,40},{64,80... | collective-permute-start | bytes 1544 | tf_op jit(solution)/shard_map/ppermute | solution.py:216
  157.1 5.1 %collective-permute-start.27 = (f32[1,128]{1,0:T(1,128)S(1)}, f32[1,128]{1,0:T(1,128)S(1)}, u32[]{:S(2)}, u32[]{:S(2)}) collective-permute-start(f32[1,128]{1,0:T(1,128)S(1)} %add.1749), channel_id=1, source_target_pairs={{0,128},{8,136},{16,144},{24,152},{32,160},{40,168},{48,176},{56,1... | collective-permute-start | bytes 1544 | tf_op jit(solution)/shard_map/ppermute | solution.py:216
  173.4 7.6 %collective-permute-start.30 = (f32[1,128]{1,0:T(1,128)S(1)}, f32[1,128]{1,0:T(1,128)S(1)}, u32[]{:S(2)}, u32[]{:S(2)}) collective-permute-start(f32[1,128]{1,0:T(1,128)S(1)} %fusion.465), channel_id=1, source_target_pairs={{0,4},{1,5},{2,6},{3,7},{4,0},{5,1},{6,2},{7,3},{8,12},{9,13},{10,... | collective-permute-start | bytes 1544 | tf_op jit(solution)/shard_map/ppermute | solution.py:216
  184.6 5.1 %collective-permute-start.32 = (f32[1,128]{1,0:T(1,128)S(1)}, f32[1,128]{1,0:T(1,128)S(1)}, u32[]{:S(2)}, u32[]{:S(2)}) collective-permute-start(f32[1,128]{1,0:T(1,128)S(1)} %add.1806), channel_id=1, source_target_pairs={{0,16},{8,24},{16,0},{24,8},{32,48},{40,56},{48,32},{56,40},{64,80... | collective-permute-start | bytes 1544 | tf_op jit(solution)/shard_map/ppermute | solution.py:216
  196.8 5.5 %collective-permute-start.35 = (f32[1,128]{1,0:T(1,128)S(1)}, f32[1,128]{1,0:T(1,128)S(1)}, u32[]{:S(2)}, u32[]{:S(2)}) collective-permute-start(f32[1,128]{1,0:T(1,128)S(1)} %add.1809), channel_id=1, source_target_pairs={{0,128},{8,136},{16,144},{24,152},{32,160},{40,168},{48,176},{56,1... | collective-permute-start | bytes 1544 | tf_op jit(solution)/shard_map/ppermute | solution.py:216
  208.2 4.6 %collective-permute-start.37 = (f32[1,128]{1,0:T(1,128)S(1)}, f32[1,128]{1,0:T(1,128)S(1)}, u32[]{:S(2)}, u32[]{:S(2)}) collective-permute-start(f32[1,128]{1,0:T(1,128)S(1)} %broadcast_add_fusion.3), channel_id=1, source_target_pairs={{0,2},{1,3},{2,0},{3,1},{4,6},{5,7},{6,4},{7,5},{8,10},{9,11},{10,... | collective-permute-start | bytes 1544 | tf_op jit(solution)/shard_map/ppermute | solution.py:216
  213.4 7.6 %collective-permute-start.38 = (f32[1,128]{1,0:T(1,128)S(1)}, f32[1,128]{1,0:T(1,128)S(1)}, u32[]{:S(2)}, u32[]{:S(2)}) collective-permute-start(f32[1,128]{1,0:T(1,128)S(1)} %fusion.464), channel_id=1, source_target_pairs={{0,4},{1,5},{2,6},{3,7},{4,0},{5,1},{6,2},{7,3},{8,12},{9,13},{10,... | collective-permute-start | bytes 1544 | tf_op jit(solution)/shard_map/ppermute | solution.py:216
  224.5 5.1 %collective-permute-start.40 = (f32[1,128]{1,0:T(1,128)S(1)}, f32[1,128]{1,0:T(1,128)S(1)}, u32[]{:S(2)}, u32[]{:S(2)}) collective-permute-start(f32[1,128]{1,0:T(1,128)S(1)} %add.1866), channel_id=1, source_target_pairs={{0,16},{8,24},{16,0},{24,8},{32,48},{40,56},{48,32},{56,40},{64,80... | collective-permute-start | bytes 1544 | tf_op jit(solution)/shard_map/ppermute | solution.py:216
  236.7 5.1 %collective-permute-start.43 = (f32[1,128]{1,0:T(1,128)S(1)}, f32[1,128]{1,0:T(1,128)S(1)}, u32[]{:S(2)}, u32[]{:S(2)}) collective-permute-start(f32[1,128]{1,0:T(1,128)S(1)} %add.1869), channel_id=1, source_target_pairs={{0,128},{8,136},{16,144},{24,152},{32,160},{40,168},{48,176},{56,1... | collective-permute-start | bytes 1544 | tf_op jit(solution)/shard_map/ppermute | solution.py:216
  252.7 7.6 %collective-permute-start.46 = (f32[1,128]{1,0:T(1,128)S(1)}, f32[1,128]{1,0:T(1,128)S(1)}, u32[]{:S(2)}, u32[]{:S(2)}) collective-permute-start(f32[1,128]{1,0:T(1,128)S(1)} %fusion.463), channel_id=1, source_target_pairs={{0,4},{1,5},{2,6},{3,7},{4,0},{5,1},{6,2},{7,3},{8,12},{9,13},{10,... | collective-permute-start | bytes 1544 | tf_op jit(solution)/shard_map/ppermute | solution.py:216
  263.8 5.1 %collective-permute-start.48 = (f32[1,128]{1,0:T(1,128)S(1)}, f32[1,128]{1,0:T(1,128)S(1)}, u32[]{:S(2)}, u32[]{:S(2)}) collective-permute-start(f32[1,128]{1,0:T(1,128)S(1)} %add.1926), channel_id=1, source_target_pairs={{0,16},{8,24},{16,0},{24,8},{32,48},{40,56},{48,32},{56,40},{64,80... | collective-permute-start | bytes 1544 | tf_op jit(solution)/shard_map/ppermute | solution.py:216
  276.2 5.1 %collective-permute-start.51 = (f32[1,128]{1,0:T(1,128)S(1)}, f32[1,128]{1,0:T(1,128)S(1)}, u32[]{:S(2)}, u32[]{:S(2)}) collective-permute-start(f32[1,128]{1,0:T(1,128)S(1)} %add.1929), channel_id=1, source_target_pairs={{0,128},{8,136},{16,144},{24,152},{32,160},{40,168},{48,176},{56,1... | collective-permute-start | bytes 1544 | tf_op jit(solution)/shard_map/ppermute | solution.py:216
  292.0 7.6 %collective-permute-start.54 = (f32[1,128]{1,0:T(1,128)S(1)}, f32[1,128]{1,0:T(1,128)S(1)}, u32[]{:S(2)}, u32[]{:S(2)}) collective-permute-start(f32[1,128]{1,0:T(1,128)S(1)} %fusion.462), channel_id=1, source_target_pairs={{0,4},{1,5},{2,6},{3,7},{4,0},{5,1},{6,2},{7,3},{8,12},{9,13},{10,... | collective-permute-start | bytes 1544 | tf_op jit(solution)/shard_map/ppermute | solution.py:216
  303.2 5.1 %collective-permute-start.56 = (f32[1,128]{1,0:T(1,128)S(1)}, f32[1,128]{1,0:T(1,128)S(1)}, u32[]{:S(2)}, u32[]{:S(2)}) collective-permute-start(f32[1,128]{1,0:T(1,128)S(1)} %add.1986), channel_id=1, source_target_pairs={{0,16},{8,24},{16,0},{24,8},{32,48},{40,56},{48,32},{56,40},{64,80... | collective-permute-start | bytes 1544 | tf_op jit(solution)/shard_map/ppermute | solution.py:216
  315.4 5.1 %collective-permute-start.59 = (f32[1,128]{1,0:T(1,128)S(1)}, f32[1,128]{1,0:T(1,128)S(1)}, u32[]{:S(2)}, u32[]{:S(2)}) collective-permute-start(f32[1,128]{1,0:T(1,128)S(1)} %add.1989), channel_id=1, source_target_pairs={{0,128},{8,136},{16,144},{24,152},{32,160},{40,168},{48,176},{56,1... | collective-permute-start | bytes 1544 | tf_op jit(solution)/shard_map/ppermute | solution.py:216
  325.6 4.6 %collective-permute-start.61 = (f32[1,128]{1,0:T(1,128)S(1)}, f32[1,128]{1,0:T(1,128)S(1)}, u32[]{:S(2)}, u32[]{:S(2)}) collective-permute-start(f32[1,128]{1,0:T(1,128)S(1)} %broadcast_add_fusion), channel_id=1, source_target_pairs={{0,2},{1,3},{2,0},{3,1},{4,6},{5,7},{6,4},{7,5},{8,10},{9,11},{10,... | collective-permute-start | bytes 1544 | tf_op jit(solution)/shard_map/ppermute | solution.py:216
  330.8 7.6 %collective-permute-start.62 = (f32[1,128]{1,0:T(1,128)S(1)}, f32[1,128]{1,0:T(1,128)S(1)}, u32[]{:S(2)}, u32[]{:S(2)}) collective-permute-start(f32[1,128]{1,0:T(1,128)S(1)} %fusion.461), channel_id=1, source_target_pairs={{0,4},{1,5},{2,6},{3,7},{4,0},{5,1},{6,2},{7,3},{8,12},{9,13},{10,... | collective-permute-start | bytes 1544 | tf_op jit(solution)/shard_map/ppermute | solution.py:216
  342.0 5.1 %collective-permute-start.64 = (f32[1,128]{1,0:T(1,128)S(1)}, f32[1,128]{1,0:T(1,128)S(1)}, u32[]{:S(2)}, u32[]{:S(2)}) collective-permute-start(f32[1,128]{1,0:T(1,128)S(1)} %add.2046), channel_id=1, source_target_pairs={{0,16},{8,24},{16,0},{24,8},{32,48},{40,56},{48,32},{56,40},{64,80... | collective-permute-start | bytes 1544 | tf_op jit(solution)/shard_map/ppermute | solution.py:216
  354.2 5.1 %collective-permute-start.67 = (f32[1,128]{1,0:T(1,128)S(1)}, f32[1,128]{1,0:T(1,128)S(1)}, u32[]{:S(2)}, u32[]{:S(2)}) collective-permute-start(f32[1,128]{1,0:T(1,128)S(1)} %add.2049), channel_id=1, source_target_pairs={{0,128},{8,136},{16,144},{24,152},{32,160},{40,168},{48,176},{56,1... | collective-permute-start | bytes 1544 | tf_op jit(solution)/shard_map/ppermute | solution.py:216
  (38 other events, 171.1 us)
